TPU v7x, 256 devices: a whole 4x4x8 slice. The times are simulated.
256 devices in a mesh: seq: 32 (over x, y, z_hi), tp: 8 (over z_lo, core).
Axes of the slice: x: 4, y: 4, z: 8 (z_hi: 2, z_lo: 4; z = z_hi * 4 + z_lo), core: 2. Of those that a mesh axis runs over, the one named last changes fastest.
Arguments:
- prefill_tokens: bfloat16 [8192, 4608], P('seq'), may hold values from -6 to 6
- decode_tokens: bfloat16 [64, 4608], replicated, may hold values from -6 to 6
- norm_gain: float32 [4608], replicated, may hold values from 0.1 to 1.9
- w_query: bfloat16 [4608, 4096], P('seq', 'tp'), may hold values from -2.1213203 to 2.1213203
- w_key: bfloat16 [4608, 2048], P('seq', 'tp'), may hold values from -0.09375 to 0.09375
- w_value: bfloat16 [4608, 2048], P('seq', 'tp'), may hold values from -0.09375 to 0.09375
- w_output: bfloat16 [4096, 4608], P('seq', 'tp'), may hold values from -0.09375 to 0.09375
- prefill_lengths: int32 [6], replicated, may hold values from 1 to 6144, 8192 in all
- context_lengths: int32 [2], replicated, may hold values from 2048 to 8192, as said below
- tail_lengths: int32 [32], replicated, may hold values from 1 to 256, as said below
- tail_slots: int32 [32], replicated, may hold values from 0 to 63, as said below
- cache_keys: bfloat16 [2, 8192, 2048], P(None, 'seq', 'tp'), may hold values from -6 to 6
- cache_values: bfloat16 [2, 8192, 2048], P(None, 'seq', 'tp'), may hold values from -6 to 6
- tail_keys: bfloat16 [64, 256, 2048], P('seq', None, 'tp'), may hold values from -6 to 6
- tail_values: bfloat16 [64, 256, 2048], P('seq', None, 'tp'), may hold values from -6 to 6
Outputs:
- prefill_out: bfloat16 [8192, 4608], P('seq', 'tp')
- decode_out: bfloat16 [64, 4608], P('seq', 'tp')
Inputs may be any that keep to these rules, and one draw needn't show every extreme that they name: `prefill_lengths`: the prompts fill all 8192 prefill tokens; the longest has exactly 6144. `context_lengths`: some prompt has exactly 8192 cached positions. `tail_lengths`: some sample has exactly 256 tail positions. `tail_slots`: distinct slot numbers; slot q lies with seq index q // 2; in every draw all slots of some seq index are used.
All inputs are finite; a program needn't handle non-finite values.
Results may differ from a plain program's by a relative error of at most 0.019.
Values may be sent and summed in bfloat16 or wider, within the bound.
No kernel may reach another device: no remote copies, remote signals or barrier semaphores. Data moves between devices by JAX's collectives and lax.ppermute only.
A program may use at most 128 MiB of HBM per device.

v0:
```python
import math

import jax
import jax.numpy as jnp
from jax import lax
from jax.sharding import PartitionSpec as P

HEAD = 128
SAMPLES = 16
NEW = 2


SOFTCAP = 50.0
QUERY_SCALE = 144.0 ** (-0.5)
NORM_EPSILON = 1e-06
ROPE_BASE = 10000.0


def combined_all(shard, axis, combine):
    everything = jax.tree.map(
        lambda part, kind: lax.all_gather(part.astype(kind), axis),
        shard,
        jax.tree.map(lambda a: jnp.bfloat16 if a.dtype == jnp.float32 else a.dtype, shard),
    )

    def take(k):
        return jax.tree.map(lambda part, own: part[k].astype(own.dtype), everything, shard)

    return lax.fori_loop(
        1, lax.axis_size(axis), lambda k, so_far: combine(so_far, take(k)), take(0)
    )


def rms_norm(inputs, norm_gain):
    values = inputs.astype(jnp.float32)
    mean_sq = jnp.mean(values * values, axis=-1, keepdims=True)
    return (values * lax.rsqrt(mean_sq + NORM_EPSILON) * norm_gain).astype(jnp.bfloat16)


def rotate(values, positions):
    half_size = values.shape[-1] // 2
    exponent = jnp.arange(half_size, dtype=jnp.float32) * (2.0 / values.shape[-1])
    frequency = ROPE_BASE ** (-exponent)
    angles = positions.astype(jnp.float32)[:, None] * frequency[None, :]
    cosine = jnp.cos(angles)[:, None, :]
    sine_part = jnp.sin(angles)[:, None, :]
    lower_half = values[..., :half_size]
    upper_half = values[..., half_size:]
    return jnp.concatenate(
        [
            lower_half * cosine - upper_half * sine_part,
            upper_half * cosine + lower_half * sine_part,
        ],
        axis=-1,
    )


def soft_cap(scores):
    return SOFTCAP * jnp.tanh(scores / SOFTCAP)


def prefill_positions(prefill_lengths, token_index):
    prompt_ends = jnp.cumsum(prefill_lengths)
    passed = token_index[:, None] >= prompt_ends[None, :]
    segment = jnp.sum(passed.astype(jnp.int32), axis=1)
    start_at = jnp.sum(jnp.where(passed, prefill_lengths[None, :], 0), axis=1)
    return (segment, token_index - start_at)


def lookup(table, indices):
    entries = jnp.arange(table.shape[0], dtype=jnp.int32)
    return jnp.sum(jnp.where(indices[:, None] == entries[None, :], table[None, :], 0), axis=1)


def combine(earlier, later):
    return (earlier[0] + later[0], earlier[1] + later[1])


def partial_softmax(scores, allowed, value_block, form):
    weights = jnp.where(allowed, jnp.exp(scores), 0.0)
    total_sum = jnp.sum(weights, axis=-1)
    mixed_out = jnp.einsum(
        form, weights.astype(jnp.bfloat16), value_block, preferred_element_type=jnp.float32
    )
    return (total_sum, mixed_out)


def shards(
    prefill_tokens,
    decode_tokens,
    norm_gain,
    w_query,
    w_key,
    w_value,
    w_output,
    prefill_lengths,
    context_lengths,
    tail_lengths,
    tail_slots,
    cache_keys,
    cache_values,
    tail_keys,
    tail_values,
):
    seq_count = lax.axis_size("seq")
    seq_index = lax.axis_index("seq")
    pf_rows = prefill_tokens.shape[0]
    dec_total = decode_tokens.shape[0]
    dec_rows = dec_total // seq_count
    q_heads = w_query.shape[1] // HEAD
    kv_heads = w_key.shape[1] // HEAD
    group_size = q_heads // kv_heads
    token_index = seq_index * pf_rows + jnp.arange(pf_rows, dtype=jnp.int32)
    query_seg, pf_positions = prefill_positions(prefill_lengths, token_index)
    row_ids = jnp.arange(dec_total, dtype=jnp.int32)
    sample_ids = row_ids // NEW
    dec_positions = (
        lookup(context_lengths, sample_ids // SAMPLES)
        + lookup(tail_lengths, sample_ids)
        + row_ids % NEW
    )
    positions = jnp.concatenate([pf_positions, dec_positions], axis=0)
    normed = rms_norm(jnp.concatenate([prefill_tokens, decode_tokens], axis=0), norm_gain)
    row_total = normed.shape[0]
    pieces = (
        lax.all_gather(w_query, "seq", axis=0, tiled=True),
        lax.all_gather(w_key, "seq", axis=0, tiled=True),
        lax.all_gather(w_value, "seq", axis=0, tiled=True),
    )
    columns = normed
    query_all, key_all, value_all = tuple(
        (jnp.dot(columns, piece_part, preferred_element_type=jnp.float32) for piece_part in pieces)
    )
    query_all = (
        rotate(query_all.reshape(row_total, q_heads, HEAD), positions) * QUERY_SCALE
    ).astype(jnp.bfloat16)
    key_all = (
        rotate(key_all.reshape(row_total, kv_heads, HEAD), positions)
        .astype(jnp.bfloat16)
        .reshape(row_total, -1)
    )
    value_all = value_all.astype(jnp.bfloat16)
    pf_query = query_all[:pf_rows].reshape(pf_rows, kv_heads, group_size, HEAD)
    pf_key = key_all[:pf_rows]
    pf_value = value_all[:pf_rows]
    query_last = token_index[pf_rows - 1]
    prompt_first = token_index[0] - pf_positions[0]
    start_state = (
        jnp.zeros((pf_rows, kv_heads, group_size), jnp.float32),
        jnp.zeros((pf_rows, kv_heads, group_size, HEAD), jnp.float32),
    )
    key_piece = lax.all_gather(pf_key, "seq", axis=0, tiled=True)
    value_piece = lax.all_gather(pf_value, "seq", axis=0, tiled=True)
    piece_len = key_piece.shape[0]
    block_len = math.gcd(512, piece_len)

    def one_block(block_step, carry_state):
        begin = block_step * block_len
        key_block = lax.dynamic_slice_in_dim(
            key_piece, block_step * block_len, block_len, 0
        ).reshape(block_len, kv_heads, HEAD)
        value_block = lax.dynamic_slice_in_dim(
            value_piece, block_step * block_len, block_len, 0
        ).reshape(block_len, kv_heads, HEAD)

        def compute(state_in):
            key_index = begin + jnp.arange(block_len, dtype=jnp.int32)
            key_seg, unused_pos = prefill_positions(prefill_lengths, key_index)
            allowed = (query_seg[:, None] == key_seg[None, :]) & (
                key_index[None, :] <= token_index[:, None]
            )
            scores = soft_cap(
                jnp.einsum(
                    "qgjd,kgd->qgjk", pf_query, key_block, preferred_element_type=jnp.float32
                )
            )
            weights = jnp.where(allowed[:, None, None, :], jnp.exp(scores), 0.0)
            total_sum = state_in[0] + jnp.sum(weights, axis=-1)
            mixed_out = state_in[1] + jnp.einsum(
                "qgjk,kgd->qgjd",
                weights.astype(jnp.bfloat16),
                value_block,
                preferred_element_type=jnp.float32,
            )
            return (total_sum, mixed_out)

        is_live = (begin <= query_last) & (begin + block_len > prompt_first)
        return lax.cond(is_live, compute, lambda state_in: state_in, carry_state)

    pf_state = lax.fori_loop(0, piece_len // block_len, one_block, start_state)
    pf_attn = (
        (pf_state[1] / pf_state[0][..., None]).astype(jnp.bfloat16).reshape(pf_rows, q_heads * HEAD)
    )
    dec_query = query_all[pf_rows:]
    dec_key = key_all[pf_rows:]
    dec_value = value_all[pf_rows:]
    prompt_count = cache_keys.shape[0]
    ctx_rows = cache_keys.shape[1]
    prompt_queries = dec_query.reshape(prompt_count, SAMPLES * NEW, kv_heads, group_size, HEAD)
    cache_k = cache_keys.reshape(prompt_count, ctx_rows, kv_heads, HEAD)
    cache_v = cache_values.reshape(prompt_count, ctx_rows, kv_heads, HEAD)
    cache_pos = seq_index * ctx_rows + jnp.arange(ctx_rows, dtype=jnp.int32)
    cache_allowed = (cache_pos[None, :] < context_lengths[:, None])[:, None, None, None, :]
    cache_scores = soft_cap(
        jnp.einsum("prgjd,pcgd->prgjc", prompt_queries, cache_k, preferred_element_type=jnp.float32)
    )
    prefix_part = partial_softmax(cache_scores, cache_allowed, cache_v, "prgjc,pcgd->prgjd")
    prefix_part = (
        prefix_part[0].reshape(dec_total, kv_heads, group_size),
        prefix_part[1].reshape(dec_total, kv_heads, group_size, HEAD),
    )
    slot_count = tail_keys.shape[0]
    tail_len = tail_keys.shape[1]
    sample_total = tail_slots.shape[0]
    local_slots = seq_index * slot_count + jnp.arange(slot_count, dtype=jnp.int32)
    owner = tail_slots[None, :] == local_slots[:, None]
    slot_queries = jnp.dot(
        owner.astype(jnp.bfloat16),
        dec_query.reshape(sample_total, NEW * q_heads * HEAD),
        preferred_element_type=jnp.float32,
    )
    slot_queries = slot_queries.astype(jnp.bfloat16).reshape(
        slot_count, NEW, kv_heads, group_size, HEAD
    )
    slot_lengths = jnp.sum(jnp.where(owner, tail_lengths[None, :], 0), axis=1)
    tail_allowed = (jnp.arange(tail_len, dtype=jnp.int32)[None, :] < slot_lengths[:, None])[
        :, None, None, None, :
    ]
    slot_keys = tail_keys.reshape(slot_count, tail_len, kv_heads, HEAD)
    slot_values = tail_values.reshape(slot_count, tail_len, kv_heads, HEAD)
    tail_scores = soft_cap(
        jnp.einsum("sngjd,stgd->sngjt", slot_queries, slot_keys, preferred_element_type=jnp.float32)
    )
    slot_part = partial_softmax(tail_scores, tail_allowed, slot_values, "sngjt,stgd->sngjd")
    owned_by = owner.T
    tail_sum = jnp.sum(jnp.where(owned_by[:, :, None, None, None], slot_part[0][None], 0.0), axis=1)
    tail_mix = jnp.sum(
        jnp.where(owned_by[:, :, None, None, None, None], slot_part[1][None], 0.0), axis=1
    )
    tail_part = (
        tail_sum.reshape(dec_total, kv_heads, group_size),
        tail_mix.reshape(dec_total, kv_heads, group_size, HEAD),
    )
    partials = combine(prefix_part, tail_part)
    combined = combined_all(partials, "seq", combine)
    merged = tuple(
        (lax.dynamic_slice_in_dim(member, seq_index * dec_rows, dec_rows, 0) for member in combined)
    )
    own_rows = seq_index * dec_rows + jnp.arange(dec_rows, dtype=jnp.int32)
    own_query = lax.dynamic_slice_in_dim(dec_query, seq_index * dec_rows, dec_rows, 0).reshape(
        dec_rows, kv_heads, group_size, HEAD
    )
    near_ids = (own_rows // NEW)[:, None] * NEW + jnp.arange(NEW, dtype=jnp.int32)[None, :]
    near_keys = jnp.take(dec_key, near_ids, axis=0).reshape(dec_rows, NEW, kv_heads, HEAD)
    near_values = jnp.take(dec_value, near_ids, axis=0).reshape(dec_rows, NEW, kv_heads, HEAD)
    near_allowed = (jnp.arange(NEW, dtype=jnp.int32)[None, :] <= (own_rows % NEW)[:, None])[
        :, None, None, :
    ]
    near_scores = soft_cap(
        jnp.einsum("rgjd,rmgd->rgjm", own_query, near_keys, preferred_element_type=jnp.float32)
    )
    near_part = partial_softmax(near_scores, near_allowed, near_values, "rgjm,rmgd->rgjd")
    finished = combine(merged, near_part)
    dec_attn = (
        (finished[1] / finished[0][..., None])
        .astype(jnp.bfloat16)
        .reshape(dec_rows, q_heads * HEAD)
    )
    attn_rows = jnp.concatenate([pf_attn, dec_attn], axis=0)
    heads_all = lax.all_gather(attn_rows, "tp", axis=1, tiled=True)
    columns = heads_all
    projected = jnp.dot(
        columns,
        lax.all_gather(w_output, "seq", axis=0, tiled=True),
        preferred_element_type=jnp.float32,
    )
    projected = projected.astype(jnp.bfloat16)
    return (projected[:pf_rows], projected[pf_rows:])


def solution(mesh):
    return jax.shard_map(
        shards,
        mesh=mesh,
        in_specs=(
            P("seq", None),
            P(),
            P(),
            P("seq", "tp"),
            P("seq", "tp"),
            P("seq", "tp"),
            P("seq", "tp"),
            P(),
            P(),
            P(),
            P(),
            P(None, "seq", "tp"),
            P(None, "seq", "tp"),
            P("seq", None, "tp"),
            P("seq", None, "tp"),
        ),
        out_specs=(P("seq", "tp"), P("seq", "tp")),
        check_vma=False,
    )
```

profile of v0, /device:TPU:2, one launch (start us, length us, event | category | flops | bytes accessed | tf_op | source)
XLA Modules:
  0.0 830.5 jit_solution(975228371402905375)
XLA Ops:
  9.5 2.5 fusion.4
  12.0 94.7 %all-gather.15.cloned.1.call-done = bf16[4608,256]{1,0:T(8,128)(2,1)} async-done(((bf16[144,256]{1,0:T(8,128)(2,1)}), bf16[4608,256]{1,0:T(8,128)(2,1)}) %all-gather.15.cloned.1.call-update) | async-done | bytes 2359312 | tf_op jit(solution)/shard_map/all_gather | solution.py:128
  106.7 2.6 convolution_convert_fusion.1
  111.3 86.3 %all-gather.9.cloned.1.call-done = bf16[4608,256]{1,0:T(8,128)(2,1)} async-done(((bf16[144,256]{1,0:T(8,128)(2,1)}), bf16[4608,256]{1,0:T(8,128)(2,1)}) %all-gather.9.cloned.1.call-update) | async-done | bytes 2359312 | tf_op jit(solution)/shard_map/all_gather | solution.py:127
  197.6 2.8 fusion.58
  202.4 1.7 reshape.524
  204.1 1.7 reshape.528
  205.8 1.7 reshape.532
  207.5 1.7 reshape.530
  210.2 101.4 %all-gather.13.cloned.1.call-done = bf16[4608,512]{1,0:T(8,128)(2,1)} async-done(((bf16[144,512]{1,0:T(8,128)(2,1)}), bf16[4608,512]{1,0:T(8,128)(2,1)}) %all-gather.13.cloned.1.call-update) | async-done | bytes 4718608 | tf_op jit(solution)/shard_map/all_gather | solution.py:126
  311.6 5.1 fusion.56
  316.7 1.3 reshape.520
  326.4 102.9 %all_gather.34 = bf16[32,64,2,2]{1,3,2,0:T(2,128)(2,1)S(1)} all-gather(bf16[1,64,2,2]{1,3,2,0:T(2,128)(2,1)S(1)} %add_convert_fusion.2), channel_id=1, replica_groups=mesh['seq'=32,'tp'=8] {'seq'}, dimensions={0}, use_global_device_ids=true | all-gather | bytes 16896 | tf_op jit(solution)/shard_map/all_gather | solution.py:21
  429.6 6.4 copy.159
  436.0 108.2 %all-gather.11.cloned.1.call-done = bf16[8192,256]{0,1:T(8,128)(2,1)} async-done(((bf16[256,256]{0,1:T(8,128)(2,1)}), bf16[8192,256]{0,1:T(8,128)(2,1)}) %all-gather.11.cloned.1.call-update) | async-done | bytes 4194320 | tf_op jit(solution)/shard_map/all_gather | solution.py:152
  544.3 26.5 %while.34 = (s32[]{:T(128)}, f32[256,2,2]{0,2,1:T(2,128)S(1)}, f32[256,2,2,128]{3,0,2,1:T(8,128)S(1)}, s32[]{:T(128)}, s32[]{:T(128)}, /*index=5*/s32[256]{0:T(2...) while((s32[]{:T(128)}, f32[256,2,2]{0,2,1:T(2,128)S(1)}, ...), condition=%wide.region_12.13_spmd.clone, body=%wide.region_6.12_spmd.clone.sunk | while | flops 271590688 | bytes 5275049 | solution.py:190
  545.0 3.1 conditional.3
  545.0 1.1 constant_dynamic-slice_fusion
  546.6 0.9 fusion.60
  548.8 3.1 conditional.3
  548.8 1.1 constant_dynamic-slice_fusion
  550.4 0.9 fusion.60
  552.6 3.1 conditional.3
  552.6 1.1 constant_dynamic-slice_fusion
  554.2 0.9 fusion.60
  556.4 3.1 conditional.3
  556.4 1.1 constant_dynamic-slice_fusion
  558.0 0.9 fusion.60
  560.2 3.1 conditional.3
  560.2 1.1 constant_dynamic-slice_fusion
  561.8 0.9 fusion.60
  571.1 62.4 %all-gather.19.cloned.1.call-done = bf16[32,64,2,2,128]{4,1,3,2,0:T(8,128)(2,1)} async-done(((bf16[1,64,2,2,128]{4,1,3,2,0:T(8,128)(2,1)}), bf16[32,64,2,2,128]{4,1,3,2,0:T(8,128)(2,1)}) %all-gather.19.cloned.1.call-update) | async-done | bytes 2097168 | tf_op jit(solution)/shard_map/all_gather | solution.py:21
  634.5 33.7 %while.33 = (s32[]{:T(128)}, f32[64,2,2]{0,2,1:T(2,128)S(1)}, f32[64,2,2,128]{3,2,1,0:T(2,128)S(1)}, bf16[32,64,2,2]{1,3,2,0:T(2,128)(2,1)S(1)}, bf16[32,64,2,2,...) while((s32[]{:T(128)}, f32[64,2,2]{0,2,1:T(2,128)S(1)}, f32[64,2,2,128]{3,2,1,0:T(2,128)S(1)}, ...), condition=%wide.region_19.20_spmd, body=%wide.region_18.19_spmd.sunk | while | flops 66053 | bytes 461447 | solution.py:29
  634.5 0.9 constant_dynamic-slice_fusion.5
  635.6 0.9 constant_dynamic-slice_fusion.5
  636.7 0.9 constant_dynamic-slice_fusion.5
  638.9 0.9 constant_dynamic-slice_fusion.5
  640.0 0.9 constant_dynamic-slice_fusion.5
  641.1 0.9 constant_dynamic-slice_fusion.5
  642.1 0.9 constant_dynamic-slice_fusion.5
  643.2 0.9 constant_dynamic-slice_fusion.5
  644.3 0.9 constant_dynamic-slice_fusion.5
  645.4 0.9 constant_dynamic-slice_fusion.5
  646.5 0.9 constant_dynamic-slice_fusion.5
  647.6 0.9 constant_dynamic-slice_fusion.5
  648.7 0.9 constant_dynamic-slice_fusion.5
  649.8 0.9 constant_dynamic-slice_fusion.5
  650.8 0.9 constant_dynamic-slice_fusion.5
  651.9 0.9 constant_dynamic-slice_fusion.5
  653.0 0.9 constant_dynamic-slice_fusion.5
  654.1 0.9 constant_dynamic-slice_fusion.5
  655.2 0.9 constant_dynamic-slice_fusion.5
  656.3 0.9 constant_dynamic-slice_fusion.5
  657.4 0.9 constant_dynamic-slice_fusion.5
  659.5 0.9 constant_dynamic-slice_fusion.5
  660.6 0.9 constant_dynamic-slice_fusion.5
  661.7 0.9 constant_dynamic-slice_fusion.5
  662.8 0.9 constant_dynamic-slice_fusion.5
  663.9 0.9 constant_dynamic-slice_fusion.5
  665.0 0.9 constant_dynamic-slice_fusion.5
  669.6 104.2 %all-gather.23.cloned.1.call-done = bf16[4096,576]{0,1:T(8,128)(2,1)} async-done(((bf16[128,576]{0,1:T(8,128)(2,1)}), bf16[4096,576]{0,1:T(8,128)(2,1)}) %all-gather.23.cloned.1.call-update) | async-done | bytes 4718608 | tf_op jit(solution)/shard_map/all_gather | solution.py:274
  773.8 42.5 %all-gather.21.cloned.1.call-done = bf16[258,4096]{0,1:T(8,128)(2,1)} async-done(((bf16[258,512]{0,1:T(8,128)(2,1)}), bf16[258,4096]{0,1:T(8,128)(2,1)}) %all-gather.21.cloned.1.call-update) | async-done | bytes 2113552 | tf_op jit(solution)/shard_map/all_gather | solution.py:270
  816.2 5.9 convolution_convert_fusion
  822.8 0.9 copy.180
  (247 shorter events, 33.8 us)
Async XLA Ops:
  7.2 99.5 %copy-start.2 = (bf16[64,4608]{1,0:T(8,128)(2,1)S(1)}, bf16[64,4608]{1,0:T(8,128)(2,1)}, u32[]{:S(2)}) copy-start(bf16[64,4608]{1,0:T(8,128)(2,1)} %param.24) | copy-start | bytes 1769476
  7.2 99.5 %copy-start = (bf16[256,4608]{1,0:T(8,128)(2,1)S(1)}, bf16[256,4608]{1,0:T(8,128)(2,1)}, u32[]{:S(2)}) copy-start(bf16[256,4608]{1,0:T(8,128)(2,1)} %param.23) | copy-start | bytes 7077892
  7.2 99.5 %copy-start.10 = (f32[4608]{0:T(1024)S(1)}, f32[4608]{0:T(1024)}, u32[]{:S(2)}) copy-start(f32[4608]{0:T(1024)} %param.25) | copy-start | bytes 55300
  7.2 99.5 %all-gather.15.cloned.1.call-start = ((), (), s32[]{:S(2)}) async-start(), calls=%async_computation.3 | async-start | bytes 2433024 | tf_op jit(solution)/shard_map/all_gather | solution.py:128
  7.9 189.6 %all-gather.9.cloned.1.call-start = ((), (), s32[]{:S(2)}) async-start(), calls=%async_computation | async-start | bytes 2433024 | tf_op jit(solution)/shard_map/all_gather | solution.py:127
  8.7 302.9 %all-gather.13.cloned.1.call-start = ((), (), s32[]{:S(2)}) async-start(), calls=%async_computation.2 | async-start | bytes 4866048 | tf_op jit(solution)/shard_map/all_gather | solution.py:126
  9.4 420.2 %all-gather.17.cloned.1.call-start = ((), (), s32[]{:S(2)}) async-start(), calls=%async_computation.4 | async-start | bytes 4325376 | tf_op jit(solution)/shard_map/all_gather | solution.py:153
  12.0 98.1 %copy-start.9 = (s32[6]{0:T(128)S(1)}, s32[6]{0:T(128)}, u32[]{:S(2)}) copy-start(s32[6]{0:T(128)} %param.30) | copy-start | bytes 76
  12.0 98.3 %copy-start.6 = (s32[2]{0:T(128)S(1)}, s32[2]{0:T(128)}, u32[]{:S(2)}) copy-start(s32[2]{0:T(128)} %param.31) | copy-start | bytes 28
  12.0 98.4 %copy-start.7 = (s32[32]{0:T(128)S(1)}, s32[32]{0:T(128)}, u32[]{:S(2)}) copy-start(s32[32]{0:T(128)} %param.32) | copy-start | bytes 388
  110.0 434.2 %all-gather.11.cloned.1.call-start = ((), (), s32[]{:S(2)}) async-start(), calls=%async_computation.1 | async-start | bytes 4325376 | tf_op jit(solution)/shard_map/all_gather | solution.py:152
  200.4 9.4 %copy-start.8 = (s32[32]{0:T(128)S(1)}, s32[32]{0:T(128)}, u32[]{:S(2)}) copy-start(s32[32]{0:T(128)} %param.33) | copy-start | bytes 388
  202.3 431.2 %all-gather.19.cloned.1.call-start = ((), (), s32[]{:S(2)}) async-start(), calls=%async_computation.5 | async-start | bytes 2162688 | tf_op jit(solution)/shard_map/all_gather | solution.py:21
  318.4 1.0 copy-start.5
  318.4 1.2 copy-start.4
  318.4 1.6 copy-start.3
  318.5 1.9 copy-start.1
  318.6 4.8 copy-start.11
  321.2 452.5 %all-gather.23.cloned.1.call-start = ((), (), s32[]{:S(2)}) async-start(), calls=%async_computation.7 | async-start | bytes 4866048 | tf_op jit(solution)/shard_map/all_gather | solution.py:274
  322.0 494.2 %all-gather.21.cloned.1.call-start = ((), (), s32[]{:S(2)}) async-start(), calls=%async_computation.6 | async-start | bytes 3538944 | tf_op jit(solution)/shard_map/all_gather | solution.py:270
Sparse Core Ops, SparseCore 0:
  11.4 95.2 all-gather.14
  110.1 87.4 all-gather.8
  201.0 110.5 all-gather.12
  314.9 105.5 all-gather.16
  423.6 120.6 all-gather.10
  548.1 85.3 all-gather.18
  636.7 136.9 all-gather.22
  775.5 40.6 all-gather.20
where the time goes:
time: 833 us; the launch traced here: 830 us
  waiting for transfers between devices  602 us (72%)
  blocking collectives  103 us (12%)
  local copies, waits for them, and re-layouts  53.7 us (6%)
  matrix products  25.6 us (3%)
  other arithmetic  18.4 us (2%)
  between operations  15.7 us (2%)
  loops' own time  11.3 us (1%)
    all_gather x1, waiting for transfers between devices, shards(): key_piece = lax.all_gather(pf_key, 'seq', axis=0, tiled=True)  108 us
    all_gather x1, waiting for transfers between devices, shards(): lax.all_gather(w_output, 'seq', axis=0, tiled=True)  104 us
    all_gather x1, blocking collectives, combined_all(): lax.all_gather(part.astype(kind), axis)  103 us
    all_gather x1, waiting for transfers between devices, shards(): lax.all_gather(w_query, 'seq', axis=0, tiled=True)  101 us
    all_gather x1, waiting for transfers between devices, shards(): lax.all_gather(w_value, 'seq', axis=0, tiled=True)  94.7 us
    all_gather x1, waiting for transfers between devices, shards(): lax.all_gather(w_key, 'seq', axis=0, tiled=True)  86.3 us
    all_gather x1, waiting for transfers between devices, combined_all(): lax.all_gather(part.astype(kind), axis)  62.4 us
    all_gather x1, waiting for transfers between devices, shards(): heads_all = lax.all_gather(attn_rows, 'tp', axis=1, tiled=True)  42.5 us
  transfers between devices with their start and end apart: 8, of which 7 were waited for; matrix products, arithmetic and copies ran while one was open for 11% of the time, Pallas kernels for 0%

commit v1 on v0

--- a/solution.py
+++ b/solution.py
@@ -16,19 +16,18 @@
 ROPE_BASE = 10000.0
 
 
-def combined_all(shard, axis, combine):
-    everything = jax.tree.map(
-        lambda part, kind: lax.all_gather(part.astype(kind), axis),
-        shard,
-        jax.tree.map(lambda a: jnp.bfloat16 if a.dtype == jnp.float32 else a.dtype, shard),
-    )
-
-    def take(k):
-        return jax.tree.map(lambda part, own: part[k].astype(own.dtype), everything, shard)
-
-    return lax.fori_loop(
-        1, lax.axis_size(axis), lambda k, so_far: combine(so_far, take(k)), take(0)
-    )
+def rows_of(x, width):
+    flat = x.reshape(-1).astype(jnp.bfloat16)
+    tile = width * 16
+    padded = -(-flat.shape[0] // tile) * tile
+    return jnp.pad(flat, (0, padded - flat.shape[0])).reshape(-1, width)
+
+
+def unrows(gathered, shape):
+    count = gathered.shape[0]
+    size = math.prod(shape)
+    flat = gathered.reshape(count, -1)[:, :size].astype(jnp.float32)
+    return jnp.sum(flat, axis=0).reshape(shape)
 
 
 def rms_norm(inputs, norm_gain):
@@ -122,15 +121,20 @@
     positions = jnp.concatenate([pf_positions, dec_positions], axis=0)
     normed = rms_norm(jnp.concatenate([prefill_tokens, decode_tokens], axis=0), norm_gain)
     row_total = normed.shape[0]
-    pieces = (
-        lax.all_gather(w_query, "seq", axis=0, tiled=True),
-        lax.all_gather(w_key, "seq", axis=0, tiled=True),
-        lax.all_gather(w_value, "seq", axis=0, tiled=True),
-    )
-    columns = normed
-    query_all, key_all, value_all = tuple(
-        (jnp.dot(columns, piece_part, preferred_element_type=jnp.float32) for piece_part in pieces)
-    )
+    q_cols = w_query.shape[1]
+    k_cols = w_key.shape[1]
+    w_rows = w_query.shape[0]
+    qkv_local = jnp.concatenate([w_query, w_key, w_value], axis=1)
+    qkv_cols = qkv_local.shape[1]
+    o_rows, o_cols = w_output.shape
+    packed_w = jnp.concatenate([qkv_local, w_output.reshape(-1, qkv_cols)], axis=0)
+    gathered_w = lax.all_gather(packed_w, "seq", axis=0)
+    w_qkv = gathered_w[:, :w_rows].reshape(seq_count * w_rows, qkv_cols)
+    w_out = gathered_w[:, w_rows:].reshape(seq_count * o_rows, o_cols)
+    qkv_all = jnp.dot(normed, w_qkv, preferred_element_type=jnp.float32)
+    query_all = qkv_all[:, :q_cols]
+    key_all = qkv_all[:, q_cols:q_cols + k_cols]
+    value_all = qkv_all[:, q_cols + k_cols:]
     query_all = (
         rotate(query_all.reshape(row_total, q_heads, HEAD), positions) * QUERY_SCALE
     ).astype(jnp.bfloat16)
@@ -143,15 +147,77 @@
     pf_query = query_all[:pf_rows].reshape(pf_rows, kv_heads, group_size, HEAD)
     pf_key = key_all[:pf_rows]
     pf_value = value_all[:pf_rows]
+    dec_query = query_all[pf_rows:]
+    dec_key = key_all[pf_rows:]
+    dec_value = value_all[pf_rows:]
+    prompt_count = cache_keys.shape[0]
+    ctx_rows = cache_keys.shape[1]
+    prompt_queries = dec_query.reshape(prompt_count, SAMPLES * NEW, kv_heads, group_size, HEAD)
+    cache_k = cache_keys.reshape(prompt_count, ctx_rows, kv_heads, HEAD)
+    cache_v = cache_values.reshape(prompt_count, ctx_rows, kv_heads, HEAD)
+    cache_pos = seq_index * ctx_rows + jnp.arange(ctx_rows, dtype=jnp.int32)
+    cache_allowed = (cache_pos[None, :] < context_lengths[:, None])[:, None, None, None, :]
+    cache_scores = soft_cap(
+        jnp.einsum("prgjd,pcgd->prgjc", prompt_queries, cache_k, preferred_element_type=jnp.float32)
+    )
+    prefix_part = partial_softmax(cache_scores, cache_allowed, cache_v, "prgjc,pcgd->prgjd")
+    prefix_part = (
+        prefix_part[0].reshape(dec_total, kv_heads, group_size),
+        prefix_part[1].reshape(dec_total, kv_heads, group_size, HEAD),
+    )
+    slot_count = tail_keys.shape[0]
+    tail_len = tail_keys.shape[1]
+    sample_total = tail_slots.shape[0]
+    local_slots = seq_index * slot_count + jnp.arange(slot_count, dtype=jnp.int32)
+    owner = tail_slots[None, :] == local_slots[:, None]
+    slot_queries = jnp.dot(
+        owner.astype(jnp.bfloat16),
+        dec_query.reshape(sample_total, NEW * q_heads * HEAD),
+        preferred_element_type=jnp.float32,
+    )
+    slot_queries = slot_queries.astype(jnp.bfloat16).reshape(
+        slot_count, NEW, kv_heads, group_size, HEAD
+    )
+    slot_lengths = jnp.sum(jnp.where(owner, tail_lengths[None, :], 0), axis=1)
+    tail_allowed = (jnp.arange(tail_len, dtype=jnp.int32)[None, :] < slot_lengths[:, None])[
+        :, None, None, None, :
+    ]
+    slot_keys = tail_keys.reshape(slot_count, tail_len, kv_heads, HEAD)
+    slot_values = tail_values.reshape(slot_count, tail_len, kv_heads, HEAD)
+    tail_scores = soft_cap(
+        jnp.einsum("sngjd,stgd->sngjt", slot_queries, slot_keys, preferred_element_type=jnp.float32)
+    )
+    slot_part = partial_softmax(tail_scores, tail_allowed, slot_values, "sngjt,stgd->sngjd")
+    owned_by = owner.T
+    tail_sum = jnp.sum(jnp.where(owned_by[:, :, None, None, None], slot_part[0][None], 0.0), axis=1)
+    tail_mix = jnp.sum(
+        jnp.where(owned_by[:, :, None, None, None, None], slot_part[1][None], 0.0), axis=1
+    )
+    tail_part = (
+        tail_sum.reshape(dec_total, kv_heads, group_size),
+        tail_mix.reshape(dec_total, kv_heads, group_size, HEAD),
+    )
+    partials = combine(prefix_part, tail_part)
+    kv_local = jnp.concatenate([pf_key, pf_value], axis=1)
+    width = kv_local.shape[1]
+    packed_kv = jnp.concatenate(
+        [kv_local, rows_of(partials[1], width), rows_of(partials[0], width)], axis=0
+    )
+    gathered_kv = lax.all_gather(packed_kv, "seq", axis=0)
+    piece_len = pf_rows * seq_count
+    key_piece = gathered_kv[:, :pf_rows, :k_cols].reshape(piece_len, k_cols)
+    value_piece = gathered_kv[:, :pf_rows, k_cols:].reshape(piece_len, k_cols)
+    mix_rows = rows_of(partials[1], width).shape[0]
+    combined = (
+        unrows(gathered_kv[:, pf_rows + mix_rows:], partials[0].shape),
+        unrows(gathered_kv[:, pf_rows:pf_rows + mix_rows], partials[1].shape),
+    )
     query_last = token_index[pf_rows - 1]
     prompt_first = token_index[0] - pf_positions[0]
     start_state = (
         jnp.zeros((pf_rows, kv_heads, group_size), jnp.float32),
         jnp.zeros((pf_rows, kv_heads, group_size, HEAD), jnp.float32),
     )
-    key_piece = lax.all_gather(pf_key, "seq", axis=0, tiled=True)
-    value_piece = lax.all_gather(pf_value, "seq", axis=0, tiled=True)
-    piece_len = key_piece.shape[0]
     block_len = math.gcd(512, piece_len)
 
     def one_block(block_step, carry_state):
@@ -191,58 +257,6 @@
     pf_attn = (
         (pf_state[1] / pf_state[0][..., None]).astype(jnp.bfloat16).reshape(pf_rows, q_heads * HEAD)
     )
-    dec_query = query_all[pf_rows:]
-    dec_key = key_all[pf_rows:]
-    dec_value = value_all[pf_rows:]
-    prompt_count = cache_keys.shape[0]
-    ctx_rows = cache_keys.shape[1]
-    prompt_queries = dec_query.reshape(prompt_count, SAMPLES * NEW, kv_heads, group_size, HEAD)
-    cache_k = cache_keys.reshape(prompt_count, ctx_rows, kv_heads, HEAD)
-    cache_v = cache_values.reshape(prompt_count, ctx_rows, kv_heads, HEAD)
-    cache_pos = seq_index * ctx_rows + jnp.arange(ctx_rows, dtype=jnp.int32)
-    cache_allowed = (cache_pos[None, :] < context_lengths[:, None])[:, None, None, None, :]
-    cache_scores = soft_cap(
-        jnp.einsum("prgjd,pcgd->prgjc", prompt_queries, cache_k, preferred_element_type=jnp.float32)
-    )
-    prefix_part = partial_softmax(cache_scores, cache_allowed, cache_v, "prgjc,pcgd->prgjd")
-    prefix_part = (
-        prefix_part[0].reshape(dec_total, kv_heads, group_size),
-        prefix_part[1].reshape(dec_total, kv_heads, group_size, HEAD),
-    )
-    slot_count = tail_keys.shape[0]
-    tail_len = tail_keys.shape[1]
-    sample_total = tail_slots.shape[0]
-    local_slots = seq_index * slot_count + jnp.arange(slot_count, dtype=jnp.int32)
-    owner = tail_slots[None, :] == local_slots[:, None]
-    slot_queries = jnp.dot(
-        owner.astype(jnp.bfloat16),
-        dec_query.reshape(sample_total, NEW * q_heads * HEAD),
-        preferred_element_type=jnp.float32,
-    )
-    slot_queries = slot_queries.astype(jnp.bfloat16).reshape(
-        slot_count, NEW, kv_heads, group_size, HEAD
-    )
-    slot_lengths = jnp.sum(jnp.where(owner, tail_lengths[None, :], 0), axis=1)
-    tail_allowed = (jnp.arange(tail_len, dtype=jnp.int32)[None, :] < slot_lengths[:, None])[
-        :, None, None, None, :
-    ]
-    slot_keys = tail_keys.reshape(slot_count, tail_len, kv_heads, HEAD)
-    slot_values = tail_values.reshape(slot_count, tail_len, kv_heads, HEAD)
-    tail_scores = soft_cap(
-        jnp.einsum("sngjd,stgd->sngjt", slot_queries, slot_keys, preferred_element_type=jnp.float32)
-    )
-    slot_part = partial_softmax(tail_scores, tail_allowed, slot_values, "sngjt,stgd->sngjd")
-    owned_by = owner.T
-    tail_sum = jnp.sum(jnp.where(owned_by[:, :, None, None, None], slot_part[0][None], 0.0), axis=1)
-    tail_mix = jnp.sum(
-        jnp.where(owned_by[:, :, None, None, None, None], slot_part[1][None], 0.0), axis=1
-    )
-    tail_part = (
-        tail_sum.reshape(dec_total, kv_heads, group_size),
-        tail_mix.reshape(dec_total, kv_heads, group_size, HEAD),
-    )
-    partials = combine(prefix_part, tail_part)
-    combined = combined_all(partials, "seq", combine)
     merged = tuple(
         (lax.dynamic_slice_in_dim(member, seq_index * dec_rows, dec_rows, 0) for member in combined)
     )
@@ -271,7 +285,7 @@
     columns = heads_all
     projected = jnp.dot(
         columns,
-        lax.all_gather(w_output, "seq", axis=0, tiled=True),
+        w_out,
         preferred_element_type=jnp.float32,
     )
     projected = projected.astype(jnp.bfloat16)

time: 833 us -> 558 us (0.67)
  waiting for transfers between devices: 602 us -> 428 us
  blocking collectives: 103 us -> 0 us
  local copies, waits for them, and re-layouts: 53.7 us -> 64.5 us
    all_gather x7 -> x2, waiting for transfers between devices: 557 us -> 377 us  [the longest x1 206 us: shards(): gathered_w = lax.all_gather(packed_w, 'seq', axis=0)]
    all_gather x1 -> x0, blocking collectives: 103 us -> none  [combined_all(): lax.all_gather(part.astype(kind), axis)]
    dynamic_slice x31 -> x0, local copies, waits for them, and re-layouts: 26.4 us -> none  [take(): part[k].astype(own.dtype)]
    reshape x0 -> x9, local copies, waits for them, and re-layouts: none -> 23.5 us  [the longest x1 10.1 us: shards(): w_out = gathered_w[:, w_rows:].reshape(seq_count * o_rows, o_cols)]
    slice x1 -> x6, local copies, waits for them, and re-layouts: 0.78 us -> 21.2 us  [the longest x1 9.06 us: shards(): w_qkv = gathered_w[:, :w_rows].reshape(seq_count * w_rows, qkv_cols)]
  transfers between devices with their start and end apart: 8 -> 3, of which waited for: 7 -> 3; matrix products, arithmetic and copies ran while one was open for 11% -> 6% of each run, Pallas kernels for 0% -> 0%
where the time goes in v1:
time: 558 us; the launch traced here: 557 us
  waiting for transfers between devices  428 us (77%)
  local copies, waits for them, and re-layouts  64.5 us (12%)
  matrix products  19.8 us (4%)
  other arithmetic  16.9 us (3%)
  between operations  15.6 us (3%)
  loops' own time  11.4 us (2%)
    all_gather x1, waiting for transfers between devices, shards(): gathered_w = lax.all_gather(packed_w, 'seq', axis=0)  206 us
    all_gather x1, waiting for transfers between devices, shards(): gathered_kv = lax.all_gather(packed_kv, 'seq', axis=0)  171 us
    all_gather x1, waiting for transfers between devices, shards(): heads_all = lax.all_gather(attn_rows, 'tp', axis=1, tiled=True)  50.7 us
  transfers between devices with their start and end apart: 3, of which 3 were waited for; matrix products, arithmetic and copies ran while one was open for 6% of the time, Pallas kernels for 0%

profile of v1, /device:TPU:2, one launch (start us, length us, event | category | flops | bytes accessed | tf_op | source)
XLA Modules:
  0.0 556.7 jit_solution(4197784397300095780)
XLA Ops:
  7.3 1.2 copy.98
  8.7 1.8 pad_maximum_fusion.2
  10.6 1.7 reshape.515
  12.3 1.0 reshape.516
  13.3 1.7 reshape.520
  15.0 1.7 reshape.521
  16.8 0.8 reduce-window.18
  17.6 0.6 and_select_fusion.1
  18.2 0.7 fusion.45
  18.9 0.7 select_reduce_fusion.1
  19.7 0.7 fusion.36
  20.4 0.9 fusion.46
  21.3 0.7 fusion.4
  22.1 0.6 iota_compare_fusion.1
  22.7 0.7 broadcast_compare_fusion
  23.3 0.6 add_rsqrt_fusion
  23.9 0.6 multiply_cosine_fusion
  24.6 206.3 %all-gather.8.cloned.1.call-done = bf16[6912,1024]{1,0:T(8,128)(2,1)} async-done(((bf16[216,1024]{1,0:T(8,128)(2,1)}), bf16[6912,1024]{1,0:T(8,128)(2,1)}) %all-gather.8.cloned.1.call-update) | async-done | bytes 14155792 | tf_op jit(solution)/shard_map/all_gather | solution.py:131
  230.9 9.1 %slice.112 = bf16[32,144,1024]{2,1,0:T(8,128)(2,1)} slice(bf16[32,216,1024]{2,1,0:T(8,128)(2,1)} %bitcast.77), slice={[0:32], [0:144], [0:1024]} | slice | bytes 18874368 | tf_op jit(solution)/shard_map/slice | solution.py:132
  239.9 7.0 %fusion.63 = (bf16[320,1024]{1,0:T(8,128)(2,1)S(1)}, f32[320,1024]{1,0:T(8,128)S(1)}) fusion(bf16[4608,1024]{1,0:T(8,128)(2,1)} %bitcast.82, f32[4608]{0:T(1024)} %param.23, f32[320]{0:T(512)} %add_rsqrt_fusion, bf16[64,4608]{1,0:T(8,128)(2,1)S(1)} %copy-done.1, bf16[256,4608]{1,0:T(8,128)(2,1)S(1)} %copy-done), kind=kOutput, calls=%fused_computation.138 | convolution fusion | flops 3030548480 | bytes 14372096 | tf_op jit(solution)/shard_map/dot_general | solution.py:134
  247.0 0.8 copy-done.5
  248.2 0.6 add_convert_fusion
  248.8 0.4 fusion.32
  249.2 0.4 fusion.59
  249.8 0.2 fusion.27
  250.2 0.3 fusion.61
  251.2 0.3 fusion.62
  252.7 0.8 pad_maximum_fusion.4
  253.7 0.6 slice.84
  254.5 0.6 fusion.60
  256.5 0.8 slice.127
  257.3 0.6 gather_fusion.1
  258.0 0.6 gather_fusion
  258.8 171.1 %all-gather.10.cloned.1.call-done = bf16[10752,512]{1,0:T(8,128)(2,1)} async-done(((bf16[336,512]{1,0:T(8,128)(2,1)}), bf16[10752,512]{1,0:T(8,128)(2,1)}) %all-gather.10.cloned.1.call-update) | async-done | bytes 11010064 | tf_op jit(solution)/shard_map/all_gather | solution.py:206
  430.0 1.9 convert_reduce_fusion.1
  431.9 1.1 slice.128
  432.9 6.0 %fusion.58 = (bf16[32,256,256]{2,1,0:T(8,128)(2,1)}, bf16[32,256,256]{2,1,0:T(8,128)(2,1)}) fusion(bf16[32,336,512]{2,1,0:T(8,128)(2,1)} %bitcast.81), kind=kLoop, calls=%fused_computation.133 | loop fusion | bytes 16777216 | tf_op jit(solution)/shard_map/slice | solution.py:209
  439.0 6.4 %copy.142 = bf16[8192,256]{0,1:T(8,128)(2,1)} copy(bf16[8192,256]{1,0:T(8,128)(2,1)} %bitcast.76) | data formatting | bytes 8388608 | tf_op jit(solution)/shard_map/reshape | solution.py:209
  445.4 6.3 %copy.141 = bf16[8192,256]{0,1:T(8,128)(2,1)} copy(bf16[8192,256]{1,0:T(8,128)(2,1)} %bitcast.75) | data formatting | bytes 8388608 | tf_op jit(solution)/shard_map/reshape | solution.py:208
  451.7 0.3 copy.148
  452.1 23.8 %while.16 = (s32[]{:T(128)}, f32[256,2,2]{0,2,1:T(2,128)S(1)}, f32[256,2,2,128]{3,0,2,1:T(8,128)S(1)}, s32[]{:T(128)}, s32[]{:T(128)}, /*index=5*/s32[256]{0:T(2...) while((s32[]{:T(128)}, f32[256,2,2]{0,2,1:T(2,128)S(1)}, ...), condition=%wide.region_17.18_spmd.clone, body=%wide.region_11.17_spmd.clone.sunk | while | flops 271590688 | bytes 5275041 | solution.py:256
  453.4 3.1 conditional.3
  454.0 1.1 constant_dynamic-slice_fusion
  455.0 0.9 fusion.57
  455.9 0.6 fusion.2
  457.3 3.1 conditional.3
  457.8 1.1 constant_dynamic-slice_fusion
  458.9 0.9 fusion.57
  459.8 0.6 fusion.2
  461.1 3.1 conditional.3
  461.6 1.1 constant_dynamic-slice_fusion
  462.7 0.9 fusion.57
  463.6 0.6 fusion.2
  464.9 3.1 conditional.3
  465.4 1.1 constant_dynamic-slice_fusion
  466.5 0.9 fusion.57
  467.4 0.6 fusion.2
  476.7 0.8 pad_maximum_fusion.3
  477.5 5.0 slice.130
  482.5 10.1 %reshape.537 = bf16[4096,576]{1,0:T(8,128)(2,1)} reshape(bf16[32,72,1024]{2,1,0:T(8,128)(2,1)} %slice.130) | data formatting | bytes 9437184 | tf_op jit(solution)/shard_map/reshape | solution.py:133
  492.6 50.7 %all-gather.6.cloned.1.call-done = bf16[258,4096]{0,1:T(8,128)(2,1)} async-done(((bf16[258,512]{0,1:T(8,128)(2,1)}), bf16[258,4096]{0,1:T(8,128)(2,1)}) %all-gather.6.cloned.1.call-update) | async-done | bytes 2113552 | tf_op jit(solution)/shard_map/all_gather | solution.py:284
  543.4 5.3 convolution_convert_fusion
  548.7 0.6 slice.132
  549.3 0.9 copy.120
  (149 shorter events, 7.2 us)
Async XLA Ops:
  7.2 15.5 %copy-start.7 = (s32[2]{0:T(128)S(1)}, s32[2]{0:T(128)}, u32[]{:S(2)}) copy-start(s32[2]{0:T(128)} %param.29) | copy-start | bytes 28
  7.2 14.8 %copy-start.8 = (s32[32]{0:T(128)S(1)}, s32[32]{0:T(128)}, u32[]{:S(2)}) copy-start(s32[32]{0:T(128)} %param.31) | copy-start | bytes 388
  7.2 14.1 %copy-start.1 = (bf16[64,4608]{1,0:T(8,128)(2,1)S(1)}, bf16[64,4608]{1,0:T(8,128)(2,1)}, u32[]{:S(2)}) copy-start(bf16[64,4608]{1,0:T(8,128)(2,1)} %param.22) | copy-start | bytes 1769476
  7.2 14.1 %copy-start = (bf16[256,4608]{1,0:T(8,128)(2,1)S(1)}, bf16[256,4608]{1,0:T(8,128)(2,1)}, u32[]{:S(2)}) copy-start(bf16[256,4608]{1,0:T(8,128)(2,1)} %param.21) | copy-start | bytes 7077892
  7.2 223.7 %all-gather.8.cloned.1.call-start = ((), (), s32[]{:S(2)}) async-start(), calls=%async_computation.1 | async-start | bytes 14598144 | tf_op jit(solution)/shard_map/all_gather | solution.py:131
  10.5 419.4 %all-gather.10.cloned.1.call-start = ((), (), s32[]{:S(2)}) async-start(), calls=%async_computation.2 | async-start | bytes 11354112 | tf_op jit(solution)/shard_map/all_gather | solution.py:206
  18.2 5.2 copy-start.10
  246.9 0.9 copy-start.5
  248.8 1.4 copy-start.4
  248.8 1.4 copy-start.6
  249.2 1.7 copy-start.9
  249.2 1.7 copy-start.11
  249.2 1.9 copy-start.3
  249.2 1.9 copy-start.13
  249.6 2.5 copy-start.2
  249.8 6.6 %copy-start.14 = (s32[2]{0:T(128)S(1)}, s32[2]{0:T(128)}, u32[]{:S(2)}) copy-start(s32[2]{0:T(128)} %get-tuple-element.399) | copy-start | bytes 28
  253.5 289.9 %all-gather.6.cloned.1.call-start = ((), (), s32[]{:S(2)}) async-start(), calls=%async_computation | async-start | bytes 3538944 | tf_op jit(solution)/shard_map/all_gather | solution.py:284
  445.4 6.7 %copy-start.12 = (s32[6]{0:T(128)S(1)}, s32[6]{0:T(128)}, u32[]{:S(2)}) copy-start(s32[6]{0:T(128)} %param.28) | copy-start | bytes 76
Sparse Core Ops, SparseCore 0:
  11.4 219.4 all-gather.7
  253.6 176.2 all-gather.9
  477.6 65.6 all-gather.5

commit v2 on v1

--- a/solution.py
+++ b/solution.py
@@ -14,6 +14,17 @@
 QUERY_SCALE = 144.0 ** (-0.5)
 NORM_EPSILON = 1e-06
 ROPE_BASE = 10000.0
+
+
+SEQ_AXES = ("sx", "sy", "sz")
+
+
+def gather_seq(block):
+    z_index = lax.axis_index("sz")
+    other = lax.ppermute(block, "sz", perm=[(0, 1), (1, 0)])
+    pair = jnp.where(z_index == 0, jnp.stack([block, other]), jnp.stack([other, block]))
+    gathered = lax.all_gather(pair, ("sx", "sy"), axis=0)
+    return gathered.reshape((-1,) + block.shape)
 
 
 def rows_of(x, width):
@@ -101,8 +112,8 @@
     tail_keys,
     tail_values,
 ):
-    seq_count = lax.axis_size("seq")
-    seq_index = lax.axis_index("seq")
+    seq_count = lax.psum(1, SEQ_AXES)
+    seq_index = lax.axis_index(SEQ_AXES)
     pf_rows = prefill_tokens.shape[0]
     dec_total = decode_tokens.shape[0]
     dec_rows = dec_total // seq_count
@@ -128,7 +139,7 @@
     qkv_cols = qkv_local.shape[1]
     o_rows, o_cols = w_output.shape
     packed_w = jnp.concatenate([qkv_local, w_output.reshape(-1, qkv_cols)], axis=0)
-    gathered_w = lax.all_gather(packed_w, "seq", axis=0)
+    gathered_w = gather_seq(packed_w)
     w_qkv = gathered_w[:, :w_rows].reshape(seq_count * w_rows, qkv_cols)
     w_out = gathered_w[:, w_rows:].reshape(seq_count * o_rows, o_cols)
     qkv_all = jnp.dot(normed, w_qkv, preferred_element_type=jnp.float32)
@@ -203,7 +214,7 @@
     packed_kv = jnp.concatenate(
         [kv_local, rows_of(partials[1], width), rows_of(partials[0], width)], axis=0
     )
-    gathered_kv = lax.all_gather(packed_kv, "seq", axis=0)
+    gathered_kv = gather_seq(packed_kv)
     piece_len = pf_rows * seq_count
     key_piece = gathered_kv[:, :pf_rows, :k_cols].reshape(piece_len, k_cols)
     value_piece = gathered_kv[:, :pf_rows, k_cols:].reshape(piece_len, k_cols)
@@ -292,27 +303,42 @@
     return (projected[:pf_rows], projected[pf_rows:])
 
 
+def seq_split(mesh):
+    column = mesh.devices[:, 0]
+    try:
+        xs = len({d.coords[0] for d in column})
+        ys = len({d.coords[1] for d in column})
+    except Exception:
+        xs, ys = 4, 4
+    return (xs, ys, column.shape[0] // (xs * ys))
+
+
 def solution(mesh):
+    split = seq_split(mesh)
+    fine = jax.sharding.Mesh(
+        mesh.devices.reshape(split + (mesh.devices.shape[1],)), SEQ_AXES + ("tp",)
+    )
+    seq = SEQ_AXES
     return jax.shard_map(
         shards,
-        mesh=mesh,
+        mesh=fine,
         in_specs=(
-            P("seq", None),
-            P(),
-            P(),
-            P("seq", "tp"),
-            P("seq", "tp"),
-            P("seq", "tp"),
-            P("seq", "tp"),
-            P(),
-            P(),
-            P(),
-            P(),
-            P(None, "seq", "tp"),
-            P(None, "seq", "tp"),
-            P("seq", None, "tp"),
-            P("seq", None, "tp"),
+            P(seq, None),
+            P(),
+            P(),
+            P(seq, "tp"),
+            P(seq, "tp"),
+            P(seq, "tp"),
+            P(seq, "tp"),
+            P(),
+            P(),
+            P(),
+            P(),
+            P(None, seq, "tp"),
+            P(None, seq, "tp"),
+            P(seq, None, "tp"),
+            P(seq, None, "tp"),
         ),
-        out_specs=(P("seq", "tp"), P("seq", "tp")),
+        out_specs=(P(seq, "tp"), P(seq, "tp")),
         check_vma=False,
     )

time: 558 us -> 408 us (0.73)
  waiting for transfers between devices: 428 us -> 269 us
  starting transfers between devices: 0.3 us -> 13.3 us
    all_gather x2, waiting for transfers between devices: 377 us -> 181 us  [gather_seq(): gathered = lax.all_gather(pair, ('sx', 'sy'), axis=0)]
    ppermute x0 -> x2, waiting for transfers between devices: none -> 27.3 us  [gather_seq(): other = lax.ppermute(block, 'sz', perm=[(0, 1), (1, 0)])]
    ppermute x0 -> x2, starting transfers between devices: none -> 13 us  [gather_seq(): other = lax.ppermute(block, 'sz', perm=[(0, 1), (1, 0)])]
    all_gather x1, waiting for transfers between devices: 50.7 us -> 60.5 us  [shards(): heads_all = lax.all_gather(attn_rows, 'tp', axis=1, tiled=True)]
  transfers between devices with their start and end apart: 3 -> 5, of which waited for: 3 -> 5; matrix products, arithmetic and copies ran while one was open for 6% -> 8% of each run, Pallas kernels for 0% -> 0%
where the time goes in v2:
time: 408 us; the launch traced here: 406 us
  waiting for transfers between devices  269 us (66%)
  local copies, waits for them, and re-layouts  62.2 us (15%)
  other arithmetic  17.1 us (4%)
  matrix products  16.8 us (4%)
  between operations  15.5 us (4%)
  starting transfers between devices  13.3 us (3%)
  loops' own time  11.4 us (3%)
    all_gather x2, waiting for transfers between devices, gather_seq(): gathered = lax.all_gather(pair, ('sx', 'sy'), axis=0)  181 us
    all_gather x1, waiting for transfers between devices, shards(): heads_all = lax.all_gather(attn_rows, 'tp', axis=1, tiled=True)  60.5 us
    ppermute x2, waiting for transfers between devices, gather_seq(): other = lax.ppermute(block, 'sz', perm=[(0, 1), (1, 0)])  27.3 us
    ppermute x2, starting transfers between devices, gather_seq(): other = lax.ppermute(block, 'sz', perm=[(0, 1), (1, 0)])  13 us
    another operation x1, loops' own time, shards(): pf_state = lax.fori_loop(0, piece_len // block_len, one_block, start_state)  11 us
    reshape x1, local copies, waits for them, and re-layouts, shards(): w_out = gathered_w[:, w_rows:].reshape(seq_count * o_rows, o_cols)  10.1 us
    slice x1, local copies, waits for them, and re-layouts, shards(): w_qkv = gathered_w[:, :w_rows].reshape(seq_count * w_rows, qkv_cols)  9.06 us
  transfers between devices with their start and end apart: 5, of which 5 were waited for; matrix products, arithmetic and copies ran while one was open for 8% of the time, Pallas kernels for 0%

profile of v2, /device:TPU:2, one launch (start us, length us, event | category | flops | bytes accessed | tf_op | source)
XLA Modules:
  0.0 405.6 jit_solution(3906543094233356279)
XLA Ops:
  7.3 1.2 copy.98
  8.5 0.2 reshape.634
  8.7 1.8 fusion.58
  10.5 7.2 %collective-permute-start = (bf16[216,1024]{1,0:T(8,128)(2,1)}, bf16[216,1024]{1,0:T(8,128)(2,1)}, u32[]{:S(2)}, u32[]{:S(2)}) collective-permute-start(bf16[216,1024]{1,0:T(8,128)(2,1)} %get-tuple-element.386), channel_id=1, source_target_pairs={{0,8},{8,0},{1,9},{9,1},{2,10},{10,2},{3,11},{11,3},{4,12},{12,4},... | collective-permute-start | bytes 1327112 | tf_op jit(solution)/shard_map/ppermute | solution.py:24
  17.7 12.7 %collective-permute-done = bf16[216,1024]{1,0:T(8,128)(2,1)} collective-permute-done((bf16[216,1024]{1,0:T(8,128)(2,1)}, bf16[216,1024]{1,0:T(8,128)(2,1)}, u32[]{:S(2)}, u32[]{:S(2)}) %collective-permute-start) | collective-permute-done | bytes 442400 | tf_op jit(solution)/shard_map/ppermute | solution.py:24
  30.4 2.2 maximum_select_fusion
  32.9 1.7 reshape.640
  34.7 1.0 reshape.641
  35.7 1.7 reshape.645
  37.4 1.7 reshape.646
  39.2 0.6 and_select_fusion.1
  40.0 0.8 fusion.46
  40.9 0.7 fusion.4
  41.5 0.7 broadcast_compare_fusion.1
  42.3 0.6 iota_compare_fusion.1
  42.9 1.3 broadcast_compare_fusion
  44.2 0.6 add_rsqrt_fusion
  44.8 0.6 multiply_cosine_fusion
  45.4 98.4 %all-gather.4.cloned.1.call-done = bf16[16,2,216,1024]{3,2,1,0:T(8,128)(2,1)} async-done(((bf16[1,2,216,1024]{3,2,1,0:T(8,128)(2,1)}), bf16[16,2,216,1024]{3,2,1,0:T(8,128)(2,1)}) %all-gather.4.cloned.1.call-update) | async-done | bytes 14155792 | tf_op jit(solution)/shard_map/all_gather | solution.py:26
  143.8 9.1 %slice.112 = bf16[32,144,1024]{2,1,0:T(8,128)(2,1)} slice(bf16[32,216,1024]{2,1,0:T(8,128)(2,1)} %bitcast.83), slice={[0:32], [0:144], [0:1024]} | slice | bytes 18874368 | tf_op jit(solution)/shard_map/slice | solution.py:143
  152.9 7.0 %fusion.65 = (bf16[320,1024]{1,0:T(8,128)(2,1)S(1)}, f32[320,1024]{1,0:T(8,128)S(1)}) fusion(bf16[4608,1024]{1,0:T(8,128)(2,1)} %bitcast.88, f32[4608]{0:T(1024)} %param.23, f32[320]{0:T(512)} %add_rsqrt_fusion, bf16[64,4608]{1,0:T(8,128)(2,1)S(1)} %copy-done.1, bf16[256,4608]{1,0:T(8,128)(2,1)S(1)} %copy-done), kind=kOutput, calls=%fused_computation.142 | convolution fusion | flops 3030548480 | bytes 14372096 | tf_op jit(solution)/shard_map/dot_general | solution.py:145
  160.0 0.8 copy-done.5
  160.8 0.2 reshape.638
  161.2 0.6 add_convert_fusion
  161.8 0.4 fusion.32
  162.2 0.4 fusion.61
  162.8 0.2 fusion.27
  163.1 0.3 fusion.63
  164.1 0.3 fusion.64
  165.7 5.8 %collective-permute-start.1 = (bf16[336,512]{1,0:T(8,128)(2,1)S(1)}, bf16[336,512]{1,0:T(8,128)(2,1)S(1)}, u32[]{:S(2)}, u32[]{:S(2)}) collective-permute-start(bf16[336,512]{1,0:T(8,128)(2,1)S(1)} %get-tuple-element.388), channel_id=1, source_target_pairs={{0,8},{8,0},{1,9},{9,1},{2,10},{10,2},{3,11},{11,3},{4,12},{12,4},... | collective-permute-start | bytes 1032200 | tf_op jit(solution)/shard_map/ppermute | solution.py:24
  171.5 14.5 %collective-permute-done.1 = bf16[336,512]{1,0:T(8,128)(2,1)S(1)} collective-permute-done((bf16[336,512]{1,0:T(8,128)(2,1)S(1)}, bf16[336,512]{1,0:T(8,128)(2,1)S(1)}, u32[]{:S(2)}, u32[]{:S(2)}) %collective-permute-start.1) | collective-permute-done | bytes 344096 | tf_op jit(solution)/shard_map/ppermute | solution.py:24
  186.1 1.0 maximum_select_fusion.1
  187.1 0.2 all-gather.8.cloned.1.call-start
  187.3 0.5 slice.84
  188.0 0.6 fusion.62
  189.9 0.8 slice.127
  190.7 0.6 gather_fusion.1
  191.4 0.6 gather_fusion
  192.0 0.2 fusion.66
  192.3 83.0 %all-gather.6.cloned.1.call-done = bf16[16,2,336,512]{3,2,1,0:T(8,128)(2,1)} async-done(((bf16[1,2,336,512]{3,2,1,0:T(8,128)(2,1)}), bf16[16,2,336,512]{3,2,1,0:T(8,128)(2,1)}) %all-gather.6.cloned.1.call-update) | async-done | bytes 11010064 | tf_op jit(solution)/shard_map/all_gather | solution.py:26
  275.3 1.9 convert_reduce_fusion.1
  277.2 1.1 slice.128
  278.3 6.0 %fusion.60 = (bf16[32,256,256]{2,1,0:T(8,128)(2,1)}, bf16[32,256,256]{2,1,0:T(8,128)(2,1)}) fusion(bf16[32,336,512]{2,1,0:T(8,128)(2,1)} %bitcast.87), kind=kLoop, calls=%fused_computation.137 | loop fusion | bytes 16777216 | tf_op jit(solution)/shard_map/slice | solution.py:220
  284.3 6.4 %copy.142 = bf16[8192,256]{0,1:T(8,128)(2,1)} copy(bf16[8192,256]{1,0:T(8,128)(2,1)} %bitcast.82) | data formatting | bytes 8388608 | tf_op jit(solution)/shard_map/reshape | solution.py:220
  290.7 6.3 %copy.141 = bf16[8192,256]{0,1:T(8,128)(2,1)} copy(bf16[8192,256]{1,0:T(8,128)(2,1)} %bitcast.81) | data formatting | bytes 8388608 | tf_op jit(solution)/shard_map/reshape | solution.py:219
  297.0 0.3 copy.148
  297.4 17.6 %while.16 = (s32[]{:T(128)}, f32[256,2,2]{0,2,1:T(2,128)S(1)}, f32[256,2,2,128]{3,0,2,1:T(8,128)S(1)}, s32[]{:T(128)}, s32[]{:T(128)}, /*index=5*/s32[256]{0:T(2...) while((s32[]{:T(128)}, f32[256,2,2]{0,2,1:T(2,128)S(1)}, ...), condition=%wide.region_17.18_spmd.clone, body=%wide.region_11.17_spmd.clone.sunk | while | flops 271590688 | bytes 5275041 | solution.py:267
  300.2 3.1 conditional.3
  300.5 0.2 compare_and_fusion
  300.7 1.1 constant_dynamic-slice_fusion
  301.8 0.9 fusion.59
  302.7 0.6 fusion.2
  304.0 3.1 conditional.3
  304.6 1.1 constant_dynamic-slice_fusion
  305.6 0.9 fusion.59
  306.5 0.6 fusion.2
  315.6 0.2 copy.143
  315.8 0.8 pad_maximum_fusion.3
  316.7 5.0 %slice.130 = bf16[32,72,1024]{2,1,0:T(8,128)(2,1)} slice(bf16[32,216,1024]{2,1,0:T(8,128)(2,1)} %bitcast.84), slice={[0:32], [144:216], [0:1024]} | slice | bytes 9437184 | tf_op jit(solution)/shard_map/slice | solution.py:144
  321.7 10.1 %reshape.663 = bf16[4096,576]{1,0:T(8,128)(2,1)} reshape(bf16[32,72,1024]{2,1,0:T(8,128)(2,1)} %slice.130) | data formatting | bytes 9437184 | tf_op jit(solution)/shard_map/reshape | solution.py:144
  331.8 60.5 %all-gather.8.cloned.1.call-done = bf16[258,4096]{0,1:T(8,128)(2,1)} async-done(((bf16[258,512]{0,1:T(8,128)(2,1)}), bf16[258,4096]{0,1:T(8,128)(2,1)}) %all-gather.8.cloned.1.call-update) | async-done | bytes 2113552 | tf_op jit(solution)/shard_map/all_gather | solution.py:295
  392.3 5.3 %convolution_convert_fusion = bf16[258,576]{1,0:T(8,128)(2,1)S(1)} fusion(bf16[258,4096]{0,1:T(8,128)(2,1)} %all-gather.8.cloned.1.call-done, bf16[4096,576]{1,0:T(8,128)(2,1)} %reshape.663), kind=kOutput, calls=%fused_computation.23 | convolution fusion | flops 1217545344 | bytes 7129344 | tf_op jit(solution)/shard_map/dot_general | solution.py:297
  397.6 0.6 slice.132
  398.2 0.9 copy.120
  (139 shorter events, 5.3 us)
Async XLA Ops:
  7.2 25.6 %copy-start.12 = (s32[6]{0:T(128)S(1)}, s32[6]{0:T(128)}, u32[]{:S(2)}) copy-start(s32[6]{0:T(128)} %param.28) | copy-start | bytes 76
  7.2 32.5 %copy-start.7 = (s32[2]{0:T(128)S(1)}, s32[2]{0:T(128)}, u32[]{:S(2)}) copy-start(s32[2]{0:T(128)} %param.29) | copy-start | bytes 28
  7.2 32.6 %copy-start.8 = (s32[32]{0:T(128)S(1)}, s32[32]{0:T(128)}, u32[]{:S(2)}) copy-start(s32[32]{0:T(128)} %param.30) | copy-start | bytes 388
  7.2 33.7 %copy-start.1 = (bf16[64,4608]{1,0:T(8,128)(2,1)S(1)}, bf16[64,4608]{1,0:T(8,128)(2,1)}, u32[]{:S(2)}) copy-start(bf16[64,4608]{1,0:T(8,128)(2,1)} %param.22) | copy-start | bytes 1769476
  7.2 33.7 %copy-start = (bf16[256,4608]{1,0:T(8,128)(2,1)S(1)}, bf16[256,4608]{1,0:T(8,128)(2,1)}, u32[]{:S(2)}) copy-start(bf16[256,4608]{1,0:T(8,128)(2,1)} %param.21) | copy-start | bytes 7077892
  7.2 136.6 %all-gather.4.cloned.1.call-start = ((), (), s32[]{:S(2)}) async-start(), calls=%async_computation | async-start | bytes 15040512 | tf_op jit(solution)/shard_map/all_gather | solution.py:26
  10.5 19.9 %collective-permute-start = (bf16[216,1024]{1,0:T(8,128)(2,1)}, bf16[216,1024]{1,0:T(8,128)(2,1)}, u32[]{:S(2)}, u32[]{:S(2)}) collective-permute-start(bf16[216,1024]{1,0:T(8,128)(2,1)} %get-tuple-element.386), channel_id=1, source_target_pairs={{0,8},{8,0},{1,9},{9,1},{2,10},{10,2},{3,11},{11,3},{4,12},{12,4},... | collective-permute-start | bytes 1327112 | tf_op jit(solution)/shard_map/ppermute | solution.py:24
  32.7 242.6 %all-gather.6.cloned.1.call-start = ((), (), s32[]{:S(2)}) async-start(), calls=%async_computation.1 | async-start | bytes 11698176 | tf_op jit(solution)/shard_map/all_gather | solution.py:26
  39.7 4.5 %copy-start.10 = (s32[2]{0:T(128)}, s32[2]{0:T(128)S(1)}, u32[]{:S(2)}) copy-start(s32[2]{0:T(128)S(1)} %get-tuple-element.404) | copy-start | bytes 28
  159.9 0.9 copy-start.5
  161.7 1.4 copy-start.4
  161.7 1.4 copy-start.6
  162.1 1.7 copy-start.9
  162.2 1.7 copy-start.11
  162.2 1.9 copy-start.3
  162.2 1.9 copy-start.14
  162.6 2.5 copy-start.2
  162.8 27.1 %copy-start.15 = (s32[2]{0:T(128)S(1)}, s32[2]{0:T(128)}, u32[]{:S(2)}) copy-start(s32[2]{0:T(128)} %get-tuple-element.403) | copy-start | bytes 28
  165.7 20.4 %collective-permute-start.1 = (bf16[336,512]{1,0:T(8,128)(2,1)S(1)}, bf16[336,512]{1,0:T(8,128)(2,1)S(1)}, u32[]{:S(2)}, u32[]{:S(2)}) collective-permute-start(bf16[336,512]{1,0:T(8,128)(2,1)S(1)} %get-tuple-element.388), channel_id=1, source_target_pairs={{0,8},{8,0},{1,9},{9,1},{2,10},{10,2},{3,11},{11,3},{4,12},{12,4},... | collective-permute-start | bytes 1032200 | tf_op jit(solution)/shard_map/ppermute | solution.py:24
  187.1 205.2 %all-gather.8.cloned.1.call-start = ((), (), s32[]{:S(2)}) async-start(), calls=%async_computation.2 | async-start | bytes 3538944 | tf_op jit(solution)/shard_map/all_gather | solution.py:295
  290.7 6.7 %copy-start.13 = (s32[6]{0:T(128)S(1)}, s32[6]{0:T(128)}, u32[]{:S(2)}) copy-start(s32[6]{0:T(128)} %param.28) | copy-start | bytes 76
Sparse Core Ops, SparseCore 0:
  32.8 110.9 all-gather.3
  187.2 88.0 all-gather.5
  316.8 75.4 all-gather.7
